TPU v7x, 32 devices: a whole 2x2x4 slice. The times are simulated.
32 devices in a mesh: panel: 2 (over y), lat: 4 (over z), lon: 4 (over x, core).
Axes of the slice: x: 2, y: 2, z: 4, core: 2. Of those that a mesh axis runs over, the one named last changes fastest.
Arguments:
- state: float32 [2, 7, 2, 256, 512], P('panel', None, None, 'lat', 'lon'), may hold values from -4 to 4
- source_slot: int32 [2, 4, 4, 768], P('panel', 'lat', 'lon'), may hold values from 0 to 3071, as said below
- donor_cell: int32 [2, 4, 4, 192], P('panel', 'lat', 'lon'), may hold values from 0 to 8000
- donor_frac: float32 [2, 4, 4, 2, 192], P('panel', 'lat', 'lon'), may hold values from 0 to 1
- donor_turn: float32 [2, 4, 4, 192], P('panel', 'lat', 'lon'), may hold values from -3.140625 to 3.140625
Outputs:
- new_state: float32 [2, 7, 2, 256, 512], P('panel', None, None, 'lat', 'lon')
Inputs may be any that keep to these rules, and one draw needn't show every extreme that they name: `source_slot`: entries name a partner panel donation (a * 4 + b) * 192 + s. For a device on an edge of its panel, the rim entries that lie on that edge name the donations that fill them; over a panel's whole border every donation of the partner panel is named exactly once. Other entries are unused.
All inputs are finite; a program needn't handle non-finite values.
Results may differ from a plain program's by a relative error of at most 0.00002.
Values sent between devices are 32-bit elements; how exact they have to be, the bound alone decides.
No kernel may reach another device: no remote copies, remote signals or barrier semaphores. Data moves between devices by JAX's collectives and lax.ppermute only.
A program may use at most 64 MiB of HBM per device.

v0:
```python
import jax
import jax.numpy as jnp
from jax import lax
from jax.sharding import PartitionSpec as P

viscosity = 0.05
resistivity = 0.05
diffusivity = 0.05
buoyancy = 0.5
time_step = 0.25
HIGHEST = lax.Precision.HIGHEST


def partner_2(block, axis, apart):
    count = lax.axis_size(axis)
    route = []
    for low in range(count):
        high = low | 1 << apart
        if high != low and high < count:
            route += [(low, high), (high, low)]
    return lax.ppermute(block, axis, route)


def shift(value, axis, step):
    size = lax.axis_size(axis)
    if step > 0:
        route = [(i, i + 1) for i in range(size - 1)]
    else:
        route = [(i + 1, i) for i in range(size - 1)]
    return lax.ppermute(value, axis, route)


def rate(up, mid, down, left, right):
    vert = jnp.concatenate([up, mid, down], axis=2)
    horz = jnp.concatenate([left, mid, right], axis=3)
    height = mid.shape[2]
    width = mid.shape[3]

    def lat_at(k):
        return vert[:, :, 2 + k : 2 + k + height, :]

    def lon_at(k):
        return horz[:, :, :, 2 + k : 2 + k + width]

    middle = mid
    d_lat = (8.0 * (lat_at(1) - lat_at(-1)) - (lat_at(2) - lat_at(-2))) / 12.0
    d_lon = (8.0 * (lon_at(1) - lon_at(-1)) - (lon_at(2) - lon_at(-2))) / 12.0
    padded = jnp.pad(middle, ((0, 0), (1, 1), (0, 0), (0, 0)))
    lap = lat_at(1) + lat_at(-1) + lon_at(1) + lon_at(-1) - 4.0 * middle
    lap = lap + padded[:, 2:] + padded[:, :-2] - 2.0 * middle
    adv_u = middle[1:2] * d_lat + middle[2:3] * d_lon
    adv_b = middle[4:5] * d_lat + middle[5:6] * d_lon
    moment = -adv_u[0:3] + adv_b[3:6] + viscosity * lap[0:3]
    induct = adv_b[0:3] - adv_u[3:6] + resistivity * lap[3:6]
    heat = -adv_u[6:7] + diffusivity * lap[6:7]
    first = moment[0:1] + buoyancy * middle[6:7]
    return jnp.concatenate([first, moment[1:3], induct, heat], axis=0)


def rotate(values, turn):
    cosine = jnp.cos(turn)
    sine = jnp.sin(turn)
    parts = [
        values[0],
        cosine * values[1] - sine * values[2],
        sine * values[1] + cosine * values[2],
        values[3],
        cosine * values[4] - sine * values[5],
        sine * values[4] + cosine * values[5],
        values[6],
    ]
    return jnp.stack(parts)


def per_device(state, source_slot, donor_cell, donor_frac, donor_turn):
    comps = state.shape[1]
    levels = state.shape[2]
    rows = state.shape[3]
    cols = state.shape[4]
    cells = donor_cell[0, 0, 0]
    frac_t = donor_frac[0, 0, 0, 0]
    frac_p = donor_frac[0, 0, 0, 1]
    turn = donor_turn[0, 0, 0]
    slots = source_slot[0, 0, 0]
    lat_pos = lax.axis_index("lat")
    lon_pos = lax.axis_index("lon")
    lat_count = lax.axis_size("lat")
    lon_count = lax.axis_size("lon")
    on_top = lat_pos == 0
    on_bottom = lat_pos == lat_count - 1
    on_left = lon_pos == 0
    on_right = lon_pos == lon_count - 1
    row = cells // (cols - 1)
    col = cells % (cols - 1)
    col_ids = jnp.arange(cols, dtype=jnp.int32)[None, :]
    row_ids = jnp.arange(rows, dtype=jnp.int32)[None, :]
    weight_lon = jnp.where(col_ids == col[:, None], (1.0 - frac_p)[:, None], 0.0) + jnp.where(
        col_ids == col[:, None] + 1, frac_p[:, None], 0.0
    )
    weight_lat = jnp.where(row_ids == row[:, None], (1.0 - frac_t)[:, None], 0.0) + jnp.where(
        row_ids == row[:, None] + 1, frac_t[:, None], 0.0
    )
    band = 2 * cols
    side = 2 * rows
    lat_slots = jnp.where(on_top, slots[0:band], slots[band : 2 * band])
    lon_slots = jnp.where(on_left, slots[2 * band : 2 * band + side], slots[2 * band + side :])
    wanted = jnp.concatenate([lat_slots, lon_slots])
    total = lax.axis_size("lat") * lax.axis_size("lon") * cells.shape[0]
    pick = (jnp.arange(total, dtype=jnp.int32)[:, None] == wanted[None, :]).astype(jnp.float32)

    def donate(field):
        flat = field.reshape(comps * levels, rows, cols)
        along = jnp.einsum("kij,sj->kis", flat, weight_lon, precision=HIGHEST)
        value = jnp.sum(along * weight_lat.T[None], axis=1)
        return rotate(value.reshape(comps, levels, -1), turn).reshape(comps * levels, -1)

    def receive(given):
        whole = lax.all_gather(given, ("lat", "lon"), axis=1, tiled=True)
        partner = partner_2(whole, "panel", 0)
        return jnp.dot(partner, pick, precision=HIGHEST)

    def section(field):
        up = shift(field[:, :, rows - 2 :, :], "lat", 1)
        down = shift(field[:, :, :2, :], "lat", -1)
        left = shift(field[:, :, :, cols - 2 :], "lon", 1)
        right = shift(field[:, :, :, :2], "lon", -1)
        rim = receive(donate(field)).reshape(comps, levels, -1)
        rim_lat = rim[:, :, :band].reshape(comps, levels, 2, cols)
        rim_lon = jnp.transpose(rim[:, :, band:].reshape(comps, levels, 2, rows), (0, 1, 3, 2))
        up = jnp.where(on_top, rim_lat, up)
        down = jnp.where(on_bottom, rim_lat, down)
        left = jnp.where(on_left, rim_lon, left)
        right = jnp.where(on_right, rim_lon, right)
        return rate(up, field, down, left, right)

    field = state[0]
    section_one = field + time_step * section(field)
    second = section(section_one)
    new_field = 0.5 * field + 0.5 * (section_one + time_step * second)
    return new_field[None]


def solution(mesh):
    in_specs = (
        P("panel", None, None, "lat", "lon"),
        P("panel", "lat", "lon", None),
        P("panel", "lat", "lon", None),
        P("panel", "lat", "lon", None, None),
        P("panel", "lat", "lon", None),
    )
    out_specs = P("panel", None, None, "lat", "lon")
    return jax.shard_map(
        per_device, mesh=mesh, in_specs=in_specs, out_specs=out_specs, check_vma=False
    )
```

profile of v0, /device:TPU:1, one launch (start us, length us, event | category | flops | bytes accessed | tf_op | source)
XLA Modules:
  0.0 83.6 jit_solution(6090372736300227283)
XLA Ops:
  0.0 0.7 broadcast_remainder_fusion
  0.7 0.7 compare_reduce_fusion
  1.4 0.8 fusion.71
  2.2 2.1 %fusion.6 = f32[14,192]{1,0:T(8,128)S(1)} fusion(f32[14,64,128]{2,1,0:T(8,128)} %bitcast.119, f32[64,192]{1,0:T(8,128)S(1)} %select_add_fusion.3, f32[192]{0:T(256)S(1)} %bitcast.153, s32[192]{0:T(256)S(1)} %get-tuple-element.50, f32[192]{0:T(256)S(1)} %broadcast_subtract_fusion.1, s32[192]{0:T(256)S(1)} %get-tuple-element.49), kind=kOutput, calls=%fused_computation.9 | convolution fusion | flops 264705408 | bytes 521728 | tf_op jit(solution)/shard_map/kij,sj->kis/dot_general | solution.py:113
  4.3 0.1 fusion.72
  4.5 23.7 %all-gather = f32[16,192,14]{1,2,0:T(8,128)S(1)} all-gather(f32[1,192,14]{1,2,0:T(8,128)S(1)} %bitcast.145), channel_id=1, replica_groups=mesh['panel'=2,'lat'=4,'lon'=4] {'lat','lon'}, dimensions={0}, use_global_device_ids=true | all-gather | bytes 182784 | tf_op jit(solution)/shard_map/all_gather | solution.py:118
  28.1 0.1 copy.18
  28.3 0.1 reshape.364
  28.4 1.3 %collective-permute-start = (f32[14,3072]{1,0:T(8,128)S(1)}, f32[14,3072]{1,0:T(8,128)S(1)}, u32[]{:S(2)}, u32[]{:S(2)}) collective-permute-start(f32[14,3072]{1,0:T(8,128)S(1)} %bitcast.127), channel_id=1, source_target_pairs={{0,16},{16,0},{1,17},{17,1},{2,18},{18,2},{3,19},{19,3},{4,20},{20... | collective-permute-start | bytes 516104 | tf_op jit(solution)/shard_map/ppermute | solution.py:21
  29.7 0.2 fusion.68
  29.9 0.0 copy-start.1
  29.9 2.4 %collective-permute-start.3 = (f32[7,2,64,2]{3,2,1,0:T(8,128)S(1)}, f32[7,2,64,2]{3,2,1,0:T(8,128)S(1)}, u32[]{:S(2)}, u32[]{:S(2)}) collective-permute-start(f32[7,2,64,2]{3,2,1,0:T(8,128)S(1)} %get-tuple-element.36), channel_id=1, source_target_pairs={{1,0},{2,1},{3,2},{5,4},{6,5},{7,6},{9,8},{10,9},{11,10},{13,12},{... | collective-permute-start | bytes 21512 | tf_op jit(solution)/shard_map/ppermute | solution.py:30
  32.3 3.2 %collective-permute-start.4 = (f32[7,2,64,2]{3,2,1,0:T(8,128)S(1)}, f32[7,2,64,2]{3,2,1,0:T(8,128)S(1)}, u32[]{:S(2)}, u32[]{:S(2)}) collective-permute-start(f32[7,2,64,2]{3,2,1,0:T(8,128)S(1)} %get-tuple-element.35), channel_id=1, source_target_pairs={{0,1},{1,2},{2,3},{4,5},{5,6},{6,7},{8,9},{9,10},{10,11},{12,13},{... | collective-permute-start | bytes 21512 | tf_op jit(solution)/shard_map/ppermute | solution.py:30
  35.5 1.3 %collective-permute-start.1 = (f32[7,2,2,128]{3,2,1,0:T(2,128)S(1)}, f32[7,2,2,128]{3,2,1,0:T(2,128)S(1)}, u32[]{:S(2)}, u32[]{:S(2)}) collective-permute-start(f32[7,2,2,128]{3,2,1,0:T(2,128)S(1)} %get-tuple-element.38), channel_id=1, source_target_pairs={{4,0},{8,4},{12,8},{5,1},{9,5},{13,9},{6,2},{10,6},{14,10},{7,3},{... | collective-permute-start | bytes 43016 | tf_op jit(solution)/shard_map/ppermute | solution.py:30
  36.8 4.0 %collective-permute-start.2 = (f32[7,2,2,128]{3,2,1,0:T(2,128)S(1)}, f32[7,2,2,128]{3,2,1,0:T(2,128)S(1)}, u32[]{:S(2)}, u32[]{:S(2)}) collective-permute-start(f32[7,2,2,128]{3,2,1,0:T(2,128)S(1)} %get-tuple-element.37), channel_id=1, source_target_pairs={{0,4},{4,8},{8,12},{1,5},{5,9},{9,13},{2,6},{6,10},{10,14},{3,7},{... | collective-permute-start | bytes 43016 | tf_op jit(solution)/shard_map/ppermute | solution.py:30
  40.9 0.0 collective-permute-done
  40.9 1.5 %fusion.1 = f32[14,384]{1,0:T(8,128)S(1)} fusion(f32[14,3072]{1,0:T(8,128)S(1)} %collective-permute-done, s32[384]{0:T(512)S(1)} %pad_add_fusion), kind=kOutput, calls=%fused_computation.2 | convolution fusion | flops 199360512 | bytes 195072 | tf_op jit(solution)/shard_map/dot_general | solution.py:120
  42.4 0.1 reshape.358
  42.5 0.2 copy.19
  42.8 0.0 collective-permute-done.4
  42.8 0.1 bitcast_select_fusion.2
  42.9 0.0 collective-permute-done.1
  43.0 0.0 collective-permute-done.2
  43.0 0.9 %multiply_add_fusion.2 = (f32[7,2,64,128]{3,2,1,0:T(8,128)S(1)}, f32[7,2,64,128]{3,2,1,0:T(8,128)S(1)}, f32[7,2,64,128]{3,2,1,0:T(8,128)S(1)}) fusion(f32[2,64,128]{2,1,0:T(8,128)S(1)} %get-tuple-element.30, f32[2,64,128]{2,1,0:T(8,128)S(1)} %get-tuple-element.31, f32[7,2,64,128]{3,2,1,0:T(8,128)S(1)} %bitcast.122, ...), kind=kLoop, calls=%fused_computation.74 | loop fusion | flops 2179072 | bytes 2009088 | tf_op jit(solution)/shard_map/add | solution.py:52
  43.9 0.6 fusion.17
  44.5 0.1 fusion.37
  44.7 0.1 maximum_multiply_fusion.1
  44.7 0.9 %fusion.66 = (f32[7,2,64,2]{3,2,1,0:T(8,128)S(1)}, f32[7,2,64,2]{3,2,1,0:T(8,128)}) fusion(f32[7,2,64,128]{3,2,1,0:T(8,128)S(1)} %get-tuple-element.28), kind=kLoop, calls=%fused_computation.175 | loop fusion | bytes 28672 | tf_op jit(solution)/shard_map/slice | solution.py:125
  45.7 1.0 %fusion.5 = f32[14,192]{1,0:T(8,128)S(1)} fusion(f32[14,64,128]{2,1,0:T(8,128)S(1)} %bitcast_add_fusion, f32[64,192]{1,0:T(8,128)S(1)} %select_add_fusion.3, f32[192]{0:T(256)S(1)} %bitcast.154, s32[192]{0:T(256)S(1)} %get-tuple-element.50, f32[192]{0:T(256)S(1)} %broadcast_subtract_fusion.1, s32[192]{0:T(256)S(1)} %get-tuple-element.49), kind=kOutput, calls=%fused_computation.8 | convolution fusion | flops 264705408 | bytes 521728 | tf_op jit(solution)/shard_map/kij,sj->kis/dot_general | solution.py:113
  46.9 18.7 %all-gather.1 = f32[16,192,14]{1,2,0:T(8,128)S(1)} all-gather(f32[1,192,14]{1,2,0:T(8,128)S(1)} %bitcast.146), channel_id=1, replica_groups=mesh['panel'=2,'lat'=4,'lon'=4] {'lat','lon'}, dimensions={0}, use_global_device_ids=true | all-gather | bytes 182784 | tf_op jit(solution)/shard_map/all_gather | solution.py:118
  65.6 0.1 copy.20
  65.7 0.1 reshape.366
  65.8 0.6 collective-permute-start.5
  66.5 2.3 %collective-permute-start.8 = (f32[7,2,64,2]{3,2,1,0:T(8,128)}, f32[7,2,64,2]{3,2,1,0:T(8,128)S(1)}, u32[]{:S(2)}, u32[]{:S(2)}) collective-permute-start(f32[7,2,64,2]{3,2,1,0:T(8,128)} %get-tuple-element.24), channel_id=1, source_target_pairs={{1,0},{2,1},{3,2},{5,4},{6,5},{7,6},{9,8},{10,9},{11,10},{13,12},{... | collective-permute-start | bytes 21512 | tf_op jit(solution)/shard_map/ppermute | solution.py:30
  68.8 3.2 %collective-permute-start.9 = (f32[7,2,64,2]{3,2,1,0:T(8,128)S(1)}, f32[7,2,64,2]{3,2,1,0:T(8,128)}, u32[]{:S(2)}, u32[]{:S(2)}) collective-permute-start(f32[7,2,64,2]{3,2,1,0:T(8,128)S(1)} %get-tuple-element.23), channel_id=1, source_target_pairs={{0,1},{1,2},{2,3},{4,5},{5,6},{6,7},{8,9},{9,10},{10,11},{12,13},{... | collective-permute-start | bytes 21512 | tf_op jit(solution)/shard_map/ppermute | solution.py:30
  72.1 1.3 %collective-permute-start.6 = (f32[7,2,2,128]{3,2,1,0:T(2,128)S(1)}, f32[7,2,2,128]{3,2,1,0:T(2,128)S(1)}, u32[]{:S(2)}, u32[]{:S(2)}) collective-permute-start(f32[7,2,2,128]{3,2,1,0:T(2,128)S(1)} %get-tuple-element.26), channel_id=1, source_target_pairs={{4,0},{8,4},{12,8},{5,1},{9,5},{13,9},{6,2},{10,6},{14,10},{7,3},{... | collective-permute-start | bytes 43016 | tf_op jit(solution)/shard_map/ppermute | solution.py:30
  73.4 4.6 %collective-permute-start.7 = (f32[7,2,2,128]{3,2,1,0:T(2,128)S(1)}, f32[7,2,2,128]{3,2,1,0:T(2,128)}, u32[]{:S(2)}, u32[]{:S(2)}) collective-permute-start(f32[7,2,2,128]{3,2,1,0:T(2,128)S(1)} %get-tuple-element.25), channel_id=1, source_target_pairs={{0,4},{4,8},{8,12},{1,5},{5,9},{9,13},{2,6},{6,10},{10,14},{3,7},{... | collective-permute-start | bytes 43016 | tf_op jit(solution)/shard_map/ppermute | solution.py:30
  78.0 1.5 %fusion = f32[14,384]{1,0:T(8,128)S(1)} fusion(f32[14,3072]{1,0:T(8,128)S(1)} %collective-permute-done.5, s32[384]{0:T(512)S(1)} %pad_add_fusion), kind=kOutput, calls=%fused_computation.1 | convolution fusion | flops 199360512 | bytes 195072 | tf_op jit(solution)/shard_map/dot_general | solution.py:120
  79.5 0.1 reshape.362
  79.6 0.2 copy.21
  79.8 0.0 collective-permute-done.8
  79.8 0.0 collective-permute-done.9
  79.8 1.1 %bitcast_select_fusion = (f32[7,2,64,2]{3,2,1,0:T(8,128)S(1)}, f32[7,2,64,2]{3,2,1,0:T(8,128)S(1)}) fusion(f32[7,2,64,2]{3,2,1,0:T(8,128)} %collective-permute-done.9, f32[7,2,2,64]{2,3,1,0:T(8,128)S(1)} %copy.21, pred[]{:T(512)S(6)} %eq.104, f32[7,2,64,2]{3,2,1,0:T(8,128)S(1)} %collective-permute-done.8, pred[]{:T(512)S(6)} %eq.107), kind=kLoop, calls=%fused_computation.67 | loop fusion | flops 3584 | bytes 35842 | tf_op jit(solution)/shard_map/jit(_where)/select_n | solution.py:132
  81.1 0.5 fusion.20
  81.6 0.9 %multiply_add_fusion = (f32[7,2,64,128]{3,2,1,0:T(8,128)S(1)}, f32[7,2,64,128]{3,2,1,0:T(8,128)S(1)}, f32[7,2,64,128]{3,2,1,0:T(8,128)S(1)}) fusion(f32[2,64,128]{2,1,0:T(8,128)S(1)} %get-tuple-element.20, f32[2,64,128]{2,1,0:T(8,128)S(1)} %get-tuple-element.18, f32[7,2,64,128]{3,2,1,0:T(8,128)S(1)} %get-tuple-element.28, ...), kind=kLoop, calls=%fused_computation.72 | loop fusion | flops 2179072 | bytes 2009088 | tf_op jit(solution)/shard_map/add | solution.py:52
  82.5 0.1 multiply_add_fusion.1
  82.6 0.1 fusion.35
  82.7 0.9 %fusion.32 = f32[1,7,2,64,128]{4,3,2,1,0:T(8,128)} fusion(f32[1,7,2,64,128]{4,3,2,1,0:T(8,128)S(1)} %copy-done, f32[1,1,2,64,128]{4,3,2,1,0:T(8,128)S(1)} %bitcast.126, f32[1,3,2,64,128]{4,3,2,1,0:T(8,128)S(1)} %bitcast.124, f32[1,2,2,64,128]{4,3,2,1,0:T(8,128)S(1)} %get-tuple-element.40, f32[1,1,2,64,128]{4,3,2,1,0:T(8,128)S(1)} %bitcast.125, ...), kind=kLoop, calls=%fused_computation.64 | loop fusion | flops 1376256 | bytes 1835008 | tf_op jit(solution)/shard_map/add | solution.py:139
  (53 shorter events, 0.6 us)
Async XLA Ops:
  0.0 4.3 %copy-start.2 = (f32[1,1,1,192]{3,2,1,0:T(1,128)S(1)}, f32[1,1,1,192]{3,2,1,0:T(1,128)}, u32[]{:S(2)}) copy-start(f32[1,1,1,192]{3,2,1,0:T(1,128)} %param.9) | copy-start | bytes 2308
  28.1 1.6 %copy-start = (f32[1,7,2,64,128]{4,3,2,1,0:T(8,128)S(1)}, f32[1,7,2,64,128]{4,3,2,1,0:T(8,128)}, u32[]{:S(2)}) copy-start(f32[1,7,2,64,128]{4,3,2,1,0:T(8,128)} %param.5) | copy-start | bytes 1376260
  28.4 12.5 %collective-permute-start = (f32[14,3072]{1,0:T(8,128)S(1)}, f32[14,3072]{1,0:T(8,128)S(1)}, u32[]{:S(2)}, u32[]{:S(2)}) collective-permute-start(f32[14,3072]{1,0:T(8,128)S(1)} %bitcast.127), channel_id=1, source_target_pairs={{0,16},{16,0},{1,17},{17,1},{2,18},{18,2},{3,19},{19,3},{4,20},{20... | collective-permute-start | bytes 516104 | tf_op jit(solution)/shard_map/ppermute | solution.py:21
  29.9 11.0 %copy-start.1 = (s32[1,1,1,768]{3,2,1,0:T(1,128)S(1)}, s32[1,1,1,768]{3,2,1,0:T(1,128)}, u32[]{:S(2)}) copy-start(s32[1,1,1,768]{3,2,1,0:T(1,128)} %param.6) | copy-start | bytes 9220
  29.9 12.9 %collective-permute-start.3 = (f32[7,2,64,2]{3,2,1,0:T(8,128)S(1)}, f32[7,2,64,2]{3,2,1,0:T(8,128)S(1)}, u32[]{:S(2)}, u32[]{:S(2)}) collective-permute-start(f32[7,2,64,2]{3,2,1,0:T(8,128)S(1)} %get-tuple-element.36), channel_id=1, source_target_pairs={{1,0},{2,1},{3,2},{5,4},{6,5},{7,6},{9,8},{10,9},{11,10},{13,12},{... | collective-permute-start | bytes 21512 | tf_op jit(solution)/shard_map/ppermute | solution.py:30
  32.3 10.5 %collective-permute-start.4 = (f32[7,2,64,2]{3,2,1,0:T(8,128)S(1)}, f32[7,2,64,2]{3,2,1,0:T(8,128)S(1)}, u32[]{:S(2)}, u32[]{:S(2)}) collective-permute-start(f32[7,2,64,2]{3,2,1,0:T(8,128)S(1)} %get-tuple-element.35), channel_id=1, source_target_pairs={{0,1},{1,2},{2,3},{4,5},{5,6},{6,7},{8,9},{9,10},{10,11},{12,13},{... | collective-permute-start | bytes 21512 | tf_op jit(solution)/shard_map/ppermute | solution.py:30
  35.5 7.5 %collective-permute-start.1 = (f32[7,2,2,128]{3,2,1,0:T(2,128)S(1)}, f32[7,2,2,128]{3,2,1,0:T(2,128)S(1)}, u32[]{:S(2)}, u32[]{:S(2)}) collective-permute-start(f32[7,2,2,128]{3,2,1,0:T(2,128)S(1)} %get-tuple-element.38), channel_id=1, source_target_pairs={{4,0},{8,4},{12,8},{5,1},{9,5},{13,9},{6,2},{10,6},{14,10},{7,3},{... | collective-permute-start | bytes 43016 | tf_op jit(solution)/shard_map/ppermute | solution.py:30
  36.8 6.2 %collective-permute-start.2 = (f32[7,2,2,128]{3,2,1,0:T(2,128)S(1)}, f32[7,2,2,128]{3,2,1,0:T(2,128)S(1)}, u32[]{:S(2)}, u32[]{:S(2)}) collective-permute-start(f32[7,2,2,128]{3,2,1,0:T(2,128)S(1)} %get-tuple-element.37), channel_id=1, source_target_pairs={{0,4},{4,8},{8,12},{1,5},{5,9},{9,13},{2,6},{6,10},{10,14},{3,7},{... | collective-permute-start | bytes 43016 | tf_op jit(solution)/shard_map/ppermute | solution.py:30
  65.8 12.1 %collective-permute-start.5 = (f32[14,3072]{1,0:T(8,128)S(1)}, f32[14,3072]{1,0:T(8,128)S(1)}, u32[]{:S(2)}, u32[]{:S(2)}) collective-permute-start(f32[14,3072]{1,0:T(8,128)S(1)} %bitcast.128), channel_id=1, source_target_pairs={{0,16},{16,0},{1,17},{17,1},{2,18},{18,2},{3,19},{19,3},{4,20},{20... | collective-permute-start | bytes 516104 | tf_op jit(solution)/shard_map/ppermute | solution.py:21
  66.5 13.3 %collective-permute-start.8 = (f32[7,2,64,2]{3,2,1,0:T(8,128)}, f32[7,2,64,2]{3,2,1,0:T(8,128)S(1)}, u32[]{:S(2)}, u32[]{:S(2)}) collective-permute-start(f32[7,2,64,2]{3,2,1,0:T(8,128)} %get-tuple-element.24), channel_id=1, source_target_pairs={{1,0},{2,1},{3,2},{5,4},{6,5},{7,6},{9,8},{10,9},{11,10},{13,12},{... | collective-permute-start | bytes 21512 | tf_op jit(solution)/shard_map/ppermute | solution.py:30
  68.8 11.0 %collective-permute-start.9 = (f32[7,2,64,2]{3,2,1,0:T(8,128)S(1)}, f32[7,2,64,2]{3,2,1,0:T(8,128)}, u32[]{:S(2)}, u32[]{:S(2)}) collective-permute-start(f32[7,2,64,2]{3,2,1,0:T(8,128)S(1)} %get-tuple-element.23), channel_id=1, source_target_pairs={{0,1},{1,2},{2,3},{4,5},{5,6},{6,7},{8,9},{9,10},{10,11},{12,13},{... | collective-permute-start | bytes 21512 | tf_op jit(solution)/shard_map/ppermute | solution.py:30
  72.1 9.0 %collective-permute-start.6 = (f32[7,2,2,128]{3,2,1,0:T(2,128)S(1)}, f32[7,2,2,128]{3,2,1,0:T(2,128)S(1)}, u32[]{:S(2)}, u32[]{:S(2)}) collective-permute-start(f32[7,2,2,128]{3,2,1,0:T(2,128)S(1)} %get-tuple-element.26), channel_id=1, source_target_pairs={{4,0},{8,4},{12,8},{5,1},{9,5},{13,9},{6,2},{10,6},{14,10},{7,3},{... | collective-permute-start | bytes 43016 | tf_op jit(solution)/shard_map/ppermute | solution.py:30
  73.4 7.7 %collective-permute-start.7 = (f32[7,2,2,128]{3,2,1,0:T(2,128)S(1)}, f32[7,2,2,128]{3,2,1,0:T(2,128)}, u32[]{:S(2)}, u32[]{:S(2)}) collective-permute-start(f32[7,2,2,128]{3,2,1,0:T(2,128)S(1)} %get-tuple-element.25), channel_id=1, source_target_pairs={{0,4},{4,8},{8,12},{1,5},{5,9},{9,13},{2,6},{6,10},{10,14},{3,7},{... | collective-permute-start | bytes 43016 | tf_op jit(solution)/shard_map/ppermute | solution.py:30
where the time goes:
time: 84.2 us; the launch traced here: 83.6 us
  blocking collectives  42.4 us (50%)
  starting transfers between devices  24.2 us (29%)
  other arithmetic  7.14 us (8%)
  matrix products  6.06 us (7%)
  local copies, waits for them, and re-layouts  3.29 us (4%)
    all_gather x2, blocking collectives, receive(): whole = lax.all_gather(given, ('lat', 'lon'), axis=1, tiled=True)  42.4 us
    ppermute x8, starting transfers between devices, shift(): return lax.ppermute(value, axis, route)  22.3 us
    dot_general x2, matrix products, donate(): along = jnp.einsum('kij,sj->kis', flat, weight_lon, precision=HIGHEST)  3.09 us
    dot_general x2, matrix products, receive(): return jnp.dot(partner, pick, precision=HIGHEST)  2.97 us
    ppermute x2, starting transfers between devices, partner_2(): return lax.ppermute(block, axis, route)  1.94 us
    add x2, other arithmetic, rate(): adv_b = middle[4:5] * d_lat + middle[5:6] * d_lon  1.8 us
  transfers between devices with their start and end apart: 10, of which 0 were waited for; matrix products, arithmetic and copies ran while one was open for 6% of the time, Pallas kernels for 0%

commit v1 on v0

--- a/solution.py
+++ b/solution.py
@@ -9,6 +9,30 @@
 buoyancy = 0.5
 time_step = 0.25
 HIGHEST = lax.Precision.HIGHEST
+
+
+def shape_column(frame_in, on_dim):
+    response = list(frame_in.shape[1:])
+    response[on_dim] *= frame_in.shape[0]
+    return jnp.moveaxis(frame_in, 0, on_dim).reshape(response)
+
+
+def streams_lift(local_values, mesh_name):
+    x_next, s_next = (lax.axis_size(mesh_name), lax.axis_index(mesh_name))
+    piece_next, extra = (local_values[None], 1)
+    while extra < x_next:
+        grid = []
+        dd = 0
+        while dd < x_next:
+            grid.append((dd, dd ^ extra))
+            dd += 1
+        frame_out = lax.ppermute(piece_next, mesh_name, grid)
+        inter = s_next & extra == 0
+        piece_next = jnp.concatenate(
+            [jnp.where(inter, piece_next, frame_out), jnp.where(inter, frame_out, piece_next)]
+        )
+        extra *= 2
+    return piece_next
 
 
 def partner_2(block, axis, apart):
@@ -115,7 +139,11 @@
         return rotate(value.reshape(comps, levels, -1), turn).reshape(comps * levels, -1)
 
     def receive(given):
-        whole = lax.all_gather(given, ("lat", "lon"), axis=1, tiled=True)
+
+        def rest_routes_all_all(out_dim, z, block_here):
+            return shape_column(streams_lift(z, block_here), out_dim)
+
+        whole = rest_routes_all_all(1, given, ("lat", "lon"))
         partner = partner_2(whole, "panel", 0)
         return jnp.dot(partner, pick, precision=HIGHEST)
 

time: 84.2 us -> 80.7 us (0.958)
  the two profiles are of different devices: /device:TPU:1 before, /device:TPU:0 now
where the time goes in v1:
time: 80.7 us; the launch traced here: 80.2 us
  starting transfers between devices  38.1 us (47%)
  waiting for transfers between devices  23.3 us (29%)
  other arithmetic  7.41 us (9%)
  matrix products  6.05 us (7%)
  local copies, waits for them, and re-layouts  4.58 us (6%)
    ppermute x8, starting transfers between devices, shift(): return lax.ppermute(value, axis, route)  22.3 us
    ppermute x8, waiting for transfers between devices, streams_lift(): frame_out = lax.ppermute(piece_next, mesh_name, grid)  15 us
    ppermute x8, starting transfers between devices, streams_lift(): frame_out = lax.ppermute(piece_next, mesh_name, grid)  12.6 us
    ppermute x2, waiting for transfers between devices, partner_2(): return lax.ppermute(block, axis, route)  8.35 us
    ppermute x2, starting transfers between devices, partner_2(): return lax.ppermute(block, axis, route)  3.17 us
    dot_general x2, matrix products, donate(): along = jnp.einsum('kij,sj->kis', flat, weight_lon, precision=HIGHEST)  3.08 us
    dot_general x2, matrix products, receive(): return jnp.dot(partner, pick, precision=HIGHEST)  2.97 us
    add x2, other arithmetic, rate(): adv_b = middle[4:5] * d_lat + middle[5:6] * d_lon  1.8 us
  transfers between devices with their start and end apart: 18, of which 7 were waited for; matrix products, arithmetic and copies ran while one was open for 8% of the time, Pallas kernels for 0%

profile of v1, /device:TPU:0, one launch (start us, length us, event | category | flops | bytes accessed | tf_op | source)
XLA Modules:
  0.0 80.2 jit_solution(12013276738112275311)
XLA Ops:
  0.0 0.8 broadcast_remainder_fusion
  0.8 0.7 compare_reduce_fusion
  1.5 0.8 fusion.71
  2.3 0.5 copy-done.9
  2.8 2.1 %fusion.6 = f32[14,192]{1,0:T(8,128)S(1)} fusion(f32[14,64,128]{2,1,0:T(8,128)} %bitcast.111, f32[64,192]{1,0:T(8,128)S(1)} %select_add_fusion.3, f32[192]{0:T(256)S(1)} %bitcast.141, s32[192]{0:T(256)S(1)} %get-tuple-element.66, f32[192]{0:T(256)S(1)} %broadcast_subtract_fusion.1, s32[192]{0:T(256)S(1)} %get-tuple-element.65), kind=kOutput, calls=%fused_computation.9 | convolution fusion | flops 264705408 | bytes 521728 | tf_op jit(solution)/shard_map/kij,sj->kis/dot_general | solution.py:137
  5.1 0.5 collective-permute-start
  5.6 0.2 fusion.68
  5.8 1.3 %collective-permute-start.7 = (f32[7,2,64,2]{3,2,1,0:T(8,128)S(1)}, f32[7,2,64,2]{3,2,1,0:T(8,128)S(1)}, u32[]{:S(2)}, u32[]{:S(2)}) collective-permute-start(f32[7,2,64,2]{3,2,1,0:T(8,128)S(1)} %get-tuple-element.36), channel_id=1, source_target_pairs={{1,0},{2,1},{3,2},{5,4},{6,5},{7,6},{9,8},{10,9},{11,10},{13,12},{... | collective-permute-start | bytes 21512 | tf_op jit(solution)/shard_map/ppermute | solution.py:54
  7.1 3.1 %collective-permute-start.8 = (f32[7,2,64,2]{3,2,1,0:T(8,128)S(1)}, f32[7,2,64,2]{3,2,1,0:T(8,128)S(1)}, u32[]{:S(2)}, u32[]{:S(2)}) collective-permute-start(f32[7,2,64,2]{3,2,1,0:T(8,128)S(1)} %get-tuple-element.35), channel_id=1, source_target_pairs={{0,1},{1,2},{2,3},{4,5},{5,6},{6,7},{8,9},{9,10},{10,11},{12,13},{... | collective-permute-start | bytes 21512 | tf_op jit(solution)/shard_map/ppermute | solution.py:54
  10.2 2.6 %collective-permute-start.1 = (f32[2,14,192]{2,1,0:T(8,128)S(1)}, f32[2,14,192]{2,1,0:T(8,128)S(1)}, u32[]{:S(2)}, u32[]{:S(2)}) collective-permute-start(f32[2,14,192]{2,1,0:T(8,128)S(1)} %pad_maximum_fusion.12), channel_id=1, source_target_pairs={{0,2},{1,3},{2,0},{3,1},{4,6},{5,7},{6,4},{7,5},{8,10},{9,11},{10,... | collective-permute-start | bytes 64520 | tf_op jit(solution)/shard_map/ppermute | solution.py:29
  12.8 1.3 %collective-permute-start.5 = (f32[7,2,2,128]{3,2,1,0:T(2,128)S(1)}, f32[7,2,2,128]{3,2,1,0:T(2,128)S(1)}, u32[]{:S(2)}, u32[]{:S(2)}) collective-permute-start(f32[7,2,2,128]{3,2,1,0:T(2,128)S(1)} %get-tuple-element.38), channel_id=1, source_target_pairs={{4,0},{8,4},{12,8},{5,1},{9,5},{13,9},{6,2},{10,6},{14,10},{7,3},{... | collective-permute-start | bytes 43016 | tf_op jit(solution)/shard_map/ppermute | solution.py:54
  14.1 5.1 %collective-permute-start.6 = (f32[7,2,2,128]{3,2,1,0:T(2,128)S(1)}, f32[7,2,2,128]{3,2,1,0:T(2,128)}, u32[]{:S(2)}, u32[]{:S(2)}) collective-permute-start(f32[7,2,2,128]{3,2,1,0:T(2,128)S(1)} %get-tuple-element.37), channel_id=1, source_target_pairs={{0,4},{4,8},{8,12},{1,5},{5,9},{9,13},{2,6},{6,10},{10,14},{3,7},{... | collective-permute-start | bytes 43016 | tf_op jit(solution)/shard_map/ppermute | solution.py:54
  19.3 1.2 %collective-permute-start.2 = (f32[4,14,192]{2,1,0:T(8,128)S(1)}, f32[4,14,192]{2,1,0:T(8,128)S(1)}, u32[]{:S(2)}, u32[]{:S(2)}) collective-permute-start(f32[4,14,192]{2,1,0:T(8,128)S(1)} %pad_maximum_fusion.10), channel_id=1, source_target_pairs={{0,4},{1,5},{2,6},{3,7},{4,0},{5,1},{6,2},{7,3},{8,12},{9,13},{10,... | collective-permute-start | bytes 129032 | tf_op jit(solution)/shard_map/ppermute | solution.py:29
  20.5 3.1 %collective-permute-done.2 = f32[4,14,192]{2,1,0:T(8,128)S(1)} collective-permute-done((f32[4,14,192]{2,1,0:T(8,128)S(1)}, f32[4,14,192]{2,1,0:T(8,128)S(1)}, u32[]{:S(2)}, u32[]{:S(2)}) %collective-permute-start.2) | collective-permute-done | bytes 43040 | tf_op jit(solution)/shard_map/ppermute | solution.py:29
  23.7 2.2 %collective-permute-start.3 = (f32[8,14,192]{2,1,0:T(8,128)S(1)}, f32[8,14,192]{2,1,0:T(8,128)S(1)}, u32[]{:S(2)}, u32[]{:S(2)}) collective-permute-start(f32[8,14,192]{2,1,0:T(8,128)S(1)} %pad_maximum_fusion.8), channel_id=1, source_target_pairs={{0,8},{1,9},{2,10},{3,11},{4,12},{5,13},{6,14},{7,15},{8,0},{9,1},... | collective-permute-start | bytes 258056 | tf_op jit(solution)/shard_map/ppermute | solution.py:29
  25.9 6.1 %collective-permute-done.3 = f32[8,14,192]{2,1,0:T(8,128)S(1)} collective-permute-done((f32[8,14,192]{2,1,0:T(8,128)S(1)}, f32[8,14,192]{2,1,0:T(8,128)S(1)}, u32[]{:S(2)}, u32[]{:S(2)}) %collective-permute-start.3) | collective-permute-done | bytes 86048 | tf_op jit(solution)/shard_map/ppermute | solution.py:29
  32.0 0.1 copy.18
  32.1 0.1 reshape.355
  32.2 1.6 %collective-permute-start.4 = (f32[14,3072]{1,0:T(8,128)S(1)}, f32[14,3072]{1,0:T(8,128)S(1)}, u32[]{:S(2)}, u32[]{:S(2)}) collective-permute-start(f32[14,3072]{1,0:T(8,128)S(1)} %reshape.355), channel_id=1, source_target_pairs={{0,16},{16,0},{1,17},{17,1},{2,18},{18,2},{3,19},{19,3},{4,20},{20... | collective-permute-start | bytes 516104 | tf_op jit(solution)/shard_map/ppermute | solution.py:45
  33.9 4.1 %collective-permute-done.4 = f32[14,3072]{1,0:T(8,128)S(1)} collective-permute-done((f32[14,3072]{1,0:T(8,128)S(1)}, f32[14,3072]{1,0:T(8,128)S(1)}, u32[]{:S(2)}, u32[]{:S(2)}) %collective-permute-start.4) | collective-permute-done | bytes 172064 | tf_op jit(solution)/shard_map/ppermute | solution.py:45
  38.0 1.5 %fusion.1 = f32[14,384]{1,0:T(8,128)S(1)} fusion(f32[14,3072]{1,0:T(8,128)S(1)} %collective-permute-done.4, s32[384]{0:T(512)S(1)} %pad_add_fusion), kind=kOutput, calls=%fused_computation.2 | convolution fusion | flops 199360512 | bytes 195072 | tf_op jit(solution)/shard_map/dot_general | solution.py:148
  39.6 0.2 copy.19
  39.9 0.1 bitcast_select_fusion.2
  40.1 0.9 %multiply_add_fusion.2 = (f32[7,2,64,128]{3,2,1,0:T(8,128)S(1)}, f32[7,2,64,128]{3,2,1,0:T(8,128)S(1)}, f32[7,2,64,128]{3,2,1,0:T(8,128)S(1)}) fusion(f32[2,64,128]{2,1,0:T(8,128)S(1)} %get-tuple-element.30, f32[2,64,128]{2,1,0:T(8,128)S(1)} %get-tuple-element.31, f32[7,2,64,128]{3,2,1,0:T(8,128)S(1)} %bitcast.114, ...), kind=kLoop, calls=%fused_computation.74 | loop fusion | flops 2179072 | bytes 2009088 | tf_op jit(solution)/shard_map/add | solution.py:76
  41.0 0.6 fusion.17
  41.9 0.7 copy-done.2
  42.7 1.0 %fusion.5 = f32[14,192]{1,0:T(8,128)S(1)} fusion(f32[14,64,128]{2,1,0:T(8,128)S(1)} %bitcast_add_fusion, f32[64,192]{1,0:T(8,128)S(1)} %copy-done.2, f32[192]{0:T(256)S(1)} %bitcast.142, s32[192]{0:T(256)S(1)} %copy-done.14, f32[192]{0:T(256)S(1)} %copy-done.10, s32[192]{0:T(256)S(1)} %copy-done.12), kind=kOutput, calls=%fused_computation.8 | convolution fusion | flops 264705408 | bytes 521728 | tf_op jit(solution)/shard_map/kij,sj->kis/dot_general | solution.py:137
  43.9 1.2 %collective-permute-done.9 = f32[1,14,192]{2,1,0:T(8,128)S(1)} collective-permute-done((f32[1,14,192]{2,1,0:T(8,128)S(1)}, f32[1,14,192]{2,1,0:T(8,128)S(1)}, u32[]{:S(2)}, u32[]{:S(2)}) %collective-permute-start.9) | collective-permute-done | bytes 10784 | tf_op jit(solution)/shard_map/ppermute | solution.py:29
  45.1 3.3 %collective-permute-start.10 = (f32[2,14,192]{2,1,0:T(8,128)S(1)}, f32[2,14,192]{2,1,0:T(8,128)S(1)}, u32[]{:S(2)}, u32[]{:S(2)}) collective-permute-start(f32[2,14,192]{2,1,0:T(8,128)S(1)} %pad_maximum_fusion.13), channel_id=1, source_target_pairs={{0,2},{1,3},{2,0},{3,1},{4,6},{5,7},{6,4},{7,5},{8,10},{9,11},{10,... | collective-permute-start | bytes 64520 | tf_op jit(solution)/shard_map/ppermute | solution.py:29
  48.4 1.9 %collective-permute-done.10 = f32[2,14,192]{2,1,0:T(8,128)S(1)} collective-permute-done((f32[2,14,192]{2,1,0:T(8,128)S(1)}, f32[2,14,192]{2,1,0:T(8,128)S(1)}, u32[]{:S(2)}, u32[]{:S(2)}) %collective-permute-start.10) | collective-permute-done | bytes 21536 | tf_op jit(solution)/shard_map/ppermute | solution.py:29
  50.3 0.7 collective-permute-start.11
  51.0 0.9 %fusion.66 = (f32[7,2,64,2]{3,2,1,0:T(8,128)S(1)}, f32[7,2,64,2]{3,2,1,0:T(8,128)}) fusion(f32[7,2,64,128]{3,2,1,0:T(8,128)S(1)} %get-tuple-element.28), kind=kLoop, calls=%fused_computation.199 | loop fusion | bytes 28672 | tf_op jit(solution)/shard_map/slice | solution.py:153
  51.9 2.7 %collective-permute-done.11 = f32[4,14,192]{2,1,0:T(8,128)S(1)} collective-permute-done((f32[4,14,192]{2,1,0:T(8,128)S(1)}, f32[4,14,192]{2,1,0:T(8,128)S(1)}, u32[]{:S(2)}, u32[]{:S(2)}) %collective-permute-start.11) | collective-permute-done | bytes 43040 | tf_op jit(solution)/shard_map/ppermute | solution.py:29
  54.7 2.1 %collective-permute-start.12 = (f32[8,14,192]{2,1,0:T(8,128)S(1)}, f32[8,14,192]{2,1,0:T(8,128)S(1)}, u32[]{:S(2)}, u32[]{:S(2)}) collective-permute-start(f32[8,14,192]{2,1,0:T(8,128)S(1)} %pad_maximum_fusion.9), channel_id=1, source_target_pairs={{0,8},{1,9},{2,10},{3,11},{4,12},{5,13},{6,14},{7,15},{8,0},{9,1},... | collective-permute-start | bytes 258056 | tf_op jit(solution)/shard_map/ppermute | solution.py:29
  56.8 1.3 %collective-permute-start.16 = (f32[7,2,64,2]{3,2,1,0:T(8,128)}, f32[7,2,64,2]{3,2,1,0:T(8,128)}, u32[]{:S(2)}, u32[]{:S(2)}) collective-permute-start(f32[7,2,64,2]{3,2,1,0:T(8,128)} %get-tuple-element.24), channel_id=1, source_target_pairs={{1,0},{2,1},{3,2},{5,4},{6,5},{7,6},{9,8},{10,9},{11,10},{13,12},{... | collective-permute-start | bytes 21512 | tf_op jit(solution)/shard_map/ppermute | solution.py:54
  58.0 3.8 %collective-permute-start.17 = (f32[7,2,64,2]{3,2,1,0:T(8,128)S(1)}, f32[7,2,64,2]{3,2,1,0:T(8,128)}, u32[]{:S(2)}, u32[]{:S(2)}) collective-permute-start(f32[7,2,64,2]{3,2,1,0:T(8,128)S(1)} %get-tuple-element.23), channel_id=1, source_target_pairs={{0,1},{1,2},{2,3},{4,5},{5,6},{6,7},{8,9},{9,10},{10,11},{12,13},{... | collective-permute-start | bytes 21512 | tf_op jit(solution)/shard_map/ppermute | solution.py:54
  61.9 1.3 %collective-permute-start.14 = (f32[7,2,2,128]{3,2,1,0:T(2,128)S(1)}, f32[7,2,2,128]{3,2,1,0:T(2,128)S(1)}, u32[]{:S(2)}, u32[]{:S(2)}) collective-permute-start(f32[7,2,2,128]{3,2,1,0:T(2,128)S(1)} %get-tuple-element.26), channel_id=1, source_target_pairs={{4,0},{8,4},{12,8},{5,1},{9,5},{13,9},{6,2},{10,6},{14,10},{7,3},{... | collective-permute-start | bytes 43016 | tf_op jit(solution)/shard_map/ppermute | solution.py:54
  63.2 5.2 %collective-permute-start.15 = (f32[7,2,2,128]{3,2,1,0:T(2,128)S(1)}, f32[7,2,2,128]{3,2,1,0:T(2,128)}, u32[]{:S(2)}, u32[]{:S(2)}) collective-permute-start(f32[7,2,2,128]{3,2,1,0:T(2,128)S(1)} %get-tuple-element.25), channel_id=1, source_target_pairs={{0,4},{4,8},{8,12},{1,5},{5,9},{9,13},{2,6},{6,10},{10,14},{3,7},{... | collective-permute-start | bytes 43016 | tf_op jit(solution)/shard_map/ppermute | solution.py:54
  68.4 0.1 copy.20
  68.5 0.1 reshape.359
  68.7 1.6 %collective-permute-start.13 = (f32[14,3072]{1,0:T(8,128)S(1)}, f32[14,3072]{1,0:T(8,128)S(1)}, u32[]{:S(2)}, u32[]{:S(2)}) collective-permute-start(f32[14,3072]{1,0:T(8,128)S(1)} %reshape.359), channel_id=1, source_target_pairs={{0,16},{16,0},{1,17},{17,1},{2,18},{18,2},{3,19},{19,3},{4,20},{20... | collective-permute-start | bytes 516104 | tf_op jit(solution)/shard_map/ppermute | solution.py:45
  70.3 4.2 %collective-permute-done.13 = f32[14,3072]{1,0:T(8,128)S(1)} collective-permute-done((f32[14,3072]{1,0:T(8,128)S(1)}, f32[14,3072]{1,0:T(8,128)S(1)}, u32[]{:S(2)}, u32[]{:S(2)}) %collective-permute-start.13) | collective-permute-done | bytes 172064 | tf_op jit(solution)/shard_map/ppermute | solution.py:45
  74.5 1.5 %fusion = f32[14,384]{1,0:T(8,128)S(1)} fusion(f32[14,3072]{1,0:T(8,128)S(1)} %collective-permute-done.13, s32[384]{0:T(512)S(1)} %copy-done.7), kind=kOutput, calls=%fused_computation.1 | convolution fusion | flops 199360512 | bytes 195072 | tf_op jit(solution)/shard_map/dot_general | solution.py:148
  76.1 0.2 copy.21
  76.4 1.1 %bitcast_select_fusion = (f32[7,2,64,2]{3,2,1,0:T(8,128)S(1)}, f32[7,2,64,2]{3,2,1,0:T(8,128)S(1)}) fusion(f32[7,2,64,2]{3,2,1,0:T(8,128)} %collective-permute-done.17, f32[7,2,2,64]{2,3,1,0:T(8,128)S(1)} %copy.21, pred[]{:T(512)S(6)} %eq.124, f32[7,2,64,2]{3,2,1,0:T(8,128)} %collective-permute-done.16, pred[]{:T(512)S(6)} %eq.127), kind=kLoop, calls=%fused_computation.67 | loop fusion | flops 3584 | bytes 35842 | tf_op jit(solution)/shard_map/jit(_where)/select_n | solution.py:160
  77.6 0.5 fusion.20
  78.1 0.9 %multiply_add_fusion = (f32[7,2,64,128]{3,2,1,0:T(8,128)S(1)}, f32[7,2,64,128]{3,2,1,0:T(8,128)S(1)}, f32[7,2,64,128]{3,2,1,0:T(8,128)S(1)}) fusion(f32[2,64,128]{2,1,0:T(8,128)S(1)} %get-tuple-element.20, f32[2,64,128]{2,1,0:T(8,128)S(1)} %get-tuple-element.18, f32[7,2,64,128]{3,2,1,0:T(8,128)S(1)} %get-tuple-element.28, ...), kind=kLoop, calls=%fused_computation.72 | loop fusion | flops 2179072 | bytes 2009088 | tf_op jit(solution)/shard_map/add | solution.py:76
  79.3 0.9 %fusion.32 = f32[1,7,2,64,128]{4,3,2,1,0:T(8,128)} fusion(f32[1,7,2,64,128]{4,3,2,1,0:T(8,128)S(1)} %copy-done, f32[1,1,2,64,128]{4,3,2,1,0:T(8,128)S(1)} %bitcast.118, f32[1,3,2,64,128]{4,3,2,1,0:T(8,128)S(1)} %bitcast.116, f32[1,2,2,64,128]{4,3,2,1,0:T(8,128)S(1)} %get-tuple-element.44, f32[1,1,2,64,128]{4,3,2,1,0:T(8,128)S(1)} %bitcast.117, ...), kind=kLoop, calls=%fused_computation.64 | loop fusion | flops 1376256 | bytes 1835008 | tf_op jit(solution)/shard_map/add | solution.py:167
  (107 shorter events, 1.6 us)
Async XLA Ops:
  0.0 5.6 %copy-start = (f32[1,7,2,64,128]{4,3,2,1,0:T(8,128)S(1)}, f32[1,7,2,64,128]{4,3,2,1,0:T(8,128)}, u32[]{:S(2)}) copy-start(f32[1,7,2,64,128]{4,3,2,1,0:T(8,128)} %param.5) | copy-start | bytes 1376260
  0.0 4.9 %copy-start.8 = (f32[1,1,1,192]{3,2,1,0:T(1,128)S(1)}, f32[1,1,1,192]{3,2,1,0:T(1,128)}, u32[]{:S(2)}) copy-start(f32[1,1,1,192]{3,2,1,0:T(1,128)} %param.9) | copy-start | bytes 2308
  2.2 2.8 %copy-start.3 = (f32[1,1,1,1,192]{4,3,2,1,0:T(1,128)}, f32[1,1,1,1,192]{4,3,2,1,0:T(1,128)S(1)}, u32[]{:S(2)}) copy-start(f32[1,1,1,1,192]{4,3,2,1,0:T(1,128)S(1)} %get-tuple-element.61) | copy-start | bytes 2308
  2.2 0.6 copy-start.9
  2.3 0.6 copy-start.11
  2.3 0.6 copy-start.13
  2.3 2.6 %copy-start.1 = (f32[64,192]{1,0:T(8,128)}, f32[64,192]{1,0:T(8,128)S(1)}, u32[]{:S(2)}) copy-start(f32[64,192]{1,0:T(8,128)S(1)} %select_add_fusion.3) | copy-start | bytes 147460
  5.1 5.1 %collective-permute-start = (f32[1,14,192]{2,1,0:T(8,128)S(1)}, f32[1,14,192]{2,1,0:T(8,128)S(1)}, u32[]{:S(2)}, u32[]{:S(2)}) collective-permute-start(f32[1,14,192]{2,1,0:T(8,128)S(1)} %broadcast_in_dim_reshape.6), channel_id=1, source_target_pairs={{0,1},{1,0},{2,3},{3,2},{4,5},{5,4},{6,7},{7,6},{8,9},{9,8},{10,11... | collective-permute-start | bytes 32264 | tf_op jit(solution)/shard_map/ppermute | solution.py:29
  5.8 34.0 %collective-permute-start.7 = (f32[7,2,64,2]{3,2,1,0:T(8,128)S(1)}, f32[7,2,64,2]{3,2,1,0:T(8,128)S(1)}, u32[]{:S(2)}, u32[]{:S(2)}) collective-permute-start(f32[7,2,64,2]{3,2,1,0:T(8,128)S(1)} %get-tuple-element.36), channel_id=1, source_target_pairs={{1,0},{2,1},{3,2},{5,4},{6,5},{7,6},{9,8},{10,9},{11,10},{13,12},{... | collective-permute-start | bytes 21512 | tf_op jit(solution)/shard_map/ppermute | solution.py:54
  7.1 32.7 %collective-permute-start.8 = (f32[7,2,64,2]{3,2,1,0:T(8,128)S(1)}, f32[7,2,64,2]{3,2,1,0:T(8,128)S(1)}, u32[]{:S(2)}, u32[]{:S(2)}) collective-permute-start(f32[7,2,64,2]{3,2,1,0:T(8,128)S(1)} %get-tuple-element.35), channel_id=1, source_target_pairs={{0,1},{1,2},{2,3},{4,5},{5,6},{6,7},{8,9},{9,10},{10,11},{12,13},{... | collective-permute-start | bytes 21512 | tf_op jit(solution)/shard_map/ppermute | solution.py:54
  10.2 9.0 %collective-permute-start.1 = (f32[2,14,192]{2,1,0:T(8,128)S(1)}, f32[2,14,192]{2,1,0:T(8,128)S(1)}, u32[]{:S(2)}, u32[]{:S(2)}) collective-permute-start(f32[2,14,192]{2,1,0:T(8,128)S(1)} %pad_maximum_fusion.12), channel_id=1, source_target_pairs={{0,2},{1,3},{2,0},{3,1},{4,6},{5,7},{6,4},{7,5},{8,10},{9,11},{10,... | collective-permute-start | bytes 64520 | tf_op jit(solution)/shard_map/ppermute | solution.py:29
  12.8 27.2 %collective-permute-start.5 = (f32[7,2,2,128]{3,2,1,0:T(2,128)S(1)}, f32[7,2,2,128]{3,2,1,0:T(2,128)S(1)}, u32[]{:S(2)}, u32[]{:S(2)}) collective-permute-start(f32[7,2,2,128]{3,2,1,0:T(2,128)S(1)} %get-tuple-element.38), channel_id=1, source_target_pairs={{4,0},{8,4},{12,8},{5,1},{9,5},{13,9},{6,2},{10,6},{14,10},{7,3},{... | collective-permute-start | bytes 43016 | tf_op jit(solution)/shard_map/ppermute | solution.py:54
  14.1 25.9 %collective-permute-start.6 = (f32[7,2,2,128]{3,2,1,0:T(2,128)S(1)}, f32[7,2,2,128]{3,2,1,0:T(2,128)}, u32[]{:S(2)}, u32[]{:S(2)}) collective-permute-start(f32[7,2,2,128]{3,2,1,0:T(2,128)S(1)} %get-tuple-element.37), channel_id=1, source_target_pairs={{0,4},{4,8},{8,12},{1,5},{5,9},{9,13},{2,6},{6,10},{10,14},{3,7},{... | collective-permute-start | bytes 43016 | tf_op jit(solution)/shard_map/ppermute | solution.py:54
  19.3 6.6 %copy-start.5 = (s32[1,1,1,768]{3,2,1,0:T(1,128)S(1)}, s32[1,1,1,768]{3,2,1,0:T(1,128)}, u32[]{:S(2)}) copy-start(s32[1,1,1,768]{3,2,1,0:T(1,128)} %param.6) | copy-start | bytes 9220
  19.3 4.3 %collective-permute-start.2 = (f32[4,14,192]{2,1,0:T(8,128)S(1)}, f32[4,14,192]{2,1,0:T(8,128)S(1)}, u32[]{:S(2)}, u32[]{:S(2)}) collective-permute-start(f32[4,14,192]{2,1,0:T(8,128)S(1)} %pad_maximum_fusion.10), channel_id=1, source_target_pairs={{0,4},{1,5},{2,6},{3,7},{4,0},{5,1},{6,2},{7,3},{8,12},{9,13},{10,... | collective-permute-start | bytes 129032 | tf_op jit(solution)/shard_map/ppermute | solution.py:29
  23.7 8.2 %collective-permute-start.3 = (f32[8,14,192]{2,1,0:T(8,128)S(1)}, f32[8,14,192]{2,1,0:T(8,128)S(1)}, u32[]{:S(2)}, u32[]{:S(2)}) collective-permute-start(f32[8,14,192]{2,1,0:T(8,128)S(1)} %pad_maximum_fusion.8), channel_id=1, source_target_pairs={{0,8},{1,9},{2,10},{3,11},{4,12},{5,13},{6,14},{7,15},{8,0},{9,1},... | collective-permute-start | bytes 258056 | tf_op jit(solution)/shard_map/ppermute | solution.py:29
  32.2 5.7 %collective-permute-start.4 = (f32[14,3072]{1,0:T(8,128)S(1)}, f32[14,3072]{1,0:T(8,128)S(1)}, u32[]{:S(2)}, u32[]{:S(2)}) collective-permute-start(f32[14,3072]{1,0:T(8,128)S(1)} %reshape.355), channel_id=1, source_target_pairs={{0,16},{16,0},{1,17},{17,1},{2,18},{18,2},{3,19},{19,3},{4,20},{20... | collective-permute-start | bytes 516104 | tf_op jit(solution)/shard_map/ppermute | solution.py:45
  33.8 4.1 %copy-start.6 = (s32[384]{0:T(512)}, s32[384]{0:T(512)S(1)}, u32[]{:S(2)}) copy-start(s32[384]{0:T(512)S(1)} %pad_add_fusion) | copy-start | bytes 4612
  41.8 0.8 %copy-start.2 = (f32[64,192]{1,0:T(8,128)S(1)}, f32[64,192]{1,0:T(8,128)}, u32[]{:S(2)}) copy-start(f32[64,192]{1,0:T(8,128)} %copy-done.1) | copy-start | bytes 147460
  41.8 0.8 %copy-start.4 = (f32[1,1,1,1,192]{4,3,2,1,0:T(1,128)S(1)}, f32[1,1,1,1,192]{4,3,2,1,0:T(1,128)}, u32[]{:S(2)}) copy-start(f32[1,1,1,1,192]{4,3,2,1,0:T(1,128)} %copy-done.3) | copy-start | bytes 2308
  41.8 0.8 %copy-start.10 = (f32[192]{0:T(256)S(1)}, f32[192]{0:T(256)}, u32[]{:S(2)}) copy-start(f32[192]{0:T(256)} %copy-done.9) | copy-start | bytes 2308
  41.8 0.8 %copy-start.12 = (s32[192]{0:T(256)S(1)}, s32[192]{0:T(256)}, u32[]{:S(2)}) copy-start(s32[192]{0:T(256)} %copy-done.11) | copy-start | bytes 2308
  41.9 0.8 %copy-start.14 = (s32[192]{0:T(256)S(1)}, s32[192]{0:T(256)}, u32[]{:S(2)}) copy-start(s32[192]{0:T(256)} %copy-done.13) | copy-start | bytes 2308
  43.8 1.2 %collective-permute-start.9 = (f32[1,14,192]{2,1,0:T(8,128)S(1)}, f32[1,14,192]{2,1,0:T(8,128)S(1)}, u32[]{:S(2)}, u32[]{:S(2)}) collective-permute-start(f32[1,14,192]{2,1,0:T(8,128)S(1)} %broadcast_in_dim_reshape.7), channel_id=1, source_target_pairs={{0,1},{1,0},{2,3},{3,2},{4,5},{5,4},{6,7},{7,6},{8,9},{9,8},{10,11... | collective-permute-start | bytes 32264 | tf_op jit(solution)/shard_map/ppermute | solution.py:29
  45.1 5.2 %collective-permute-start.10 = (f32[2,14,192]{2,1,0:T(8,128)S(1)}, f32[2,14,192]{2,1,0:T(8,128)S(1)}, u32[]{:S(2)}, u32[]{:S(2)}) collective-permute-start(f32[2,14,192]{2,1,0:T(8,128)S(1)} %pad_maximum_fusion.13), channel_id=1, source_target_pairs={{0,2},{1,3},{2,0},{3,1},{4,6},{5,7},{6,4},{7,5},{8,10},{9,11},{10,... | collective-permute-start | bytes 64520 | tf_op jit(solution)/shard_map/ppermute | solution.py:29
  50.3 4.3 %collective-permute-start.11 = (f32[4,14,192]{2,1,0:T(8,128)S(1)}, f32[4,14,192]{2,1,0:T(8,128)S(1)}, u32[]{:S(2)}, u32[]{:S(2)}) collective-permute-start(f32[4,14,192]{2,1,0:T(8,128)S(1)} %pad_maximum_fusion.11), channel_id=1, source_target_pairs={{0,4},{1,5},{2,6},{3,7},{4,0},{5,1},{6,2},{7,3},{8,12},{9,13},{10,... | collective-permute-start | bytes 129032 | tf_op jit(solution)/shard_map/ppermute | solution.py:29
  54.7 13.7 %collective-permute-start.12 = (f32[8,14,192]{2,1,0:T(8,128)S(1)}, f32[8,14,192]{2,1,0:T(8,128)S(1)}, u32[]{:S(2)}, u32[]{:S(2)}) collective-permute-start(f32[8,14,192]{2,1,0:T(8,128)S(1)} %pad_maximum_fusion.9), channel_id=1, source_target_pairs={{0,8},{1,9},{2,10},{3,11},{4,12},{5,13},{6,14},{7,15},{8,0},{9,1},... | collective-permute-start | bytes 258056 | tf_op jit(solution)/shard_map/ppermute | solution.py:29
  56.8 19.6 %collective-permute-start.16 = (f32[7,2,64,2]{3,2,1,0:T(8,128)}, f32[7,2,64,2]{3,2,1,0:T(8,128)}, u32[]{:S(2)}, u32[]{:S(2)}) collective-permute-start(f32[7,2,64,2]{3,2,1,0:T(8,128)} %get-tuple-element.24), channel_id=1, source_target_pairs={{1,0},{2,1},{3,2},{5,4},{6,5},{7,6},{9,8},{10,9},{11,10},{13,12},{... | collective-permute-start | bytes 21512 | tf_op jit(solution)/shard_map/ppermute | solution.py:54
  58.0 18.3 %collective-permute-start.17 = (f32[7,2,64,2]{3,2,1,0:T(8,128)S(1)}, f32[7,2,64,2]{3,2,1,0:T(8,128)}, u32[]{:S(2)}, u32[]{:S(2)}) collective-permute-start(f32[7,2,64,2]{3,2,1,0:T(8,128)S(1)} %get-tuple-element.23), channel_id=1, source_target_pairs={{0,1},{1,2},{2,3},{4,5},{5,6},{6,7},{8,9},{9,10},{10,11},{12,13},{... | collective-permute-start | bytes 21512 | tf_op jit(solution)/shard_map/ppermute | solution.py:54
  61.9 15.7 %collective-permute-start.14 = (f32[7,2,2,128]{3,2,1,0:T(2,128)S(1)}, f32[7,2,2,128]{3,2,1,0:T(2,128)S(1)}, u32[]{:S(2)}, u32[]{:S(2)}) collective-permute-start(f32[7,2,2,128]{3,2,1,0:T(2,128)S(1)} %get-tuple-element.26), channel_id=1, source_target_pairs={{4,0},{8,4},{12,8},{5,1},{9,5},{13,9},{6,2},{10,6},{14,10},{7,3},{... | collective-permute-start | bytes 43016 | tf_op jit(solution)/shard_map/ppermute | solution.py:54
  63.2 14.4 %collective-permute-start.15 = (f32[7,2,2,128]{3,2,1,0:T(2,128)S(1)}, f32[7,2,2,128]{3,2,1,0:T(2,128)}, u32[]{:S(2)}, u32[]{:S(2)}) collective-permute-start(f32[7,2,2,128]{3,2,1,0:T(2,128)S(1)} %get-tuple-element.25), channel_id=1, source_target_pairs={{0,4},{4,8},{8,12},{1,5},{5,9},{9,13},{2,6},{6,10},{10,14},{3,7},{... | collective-permute-start | bytes 43016 | tf_op jit(solution)/shard_map/ppermute | solution.py:54
  68.5 6.0 %copy-start.7 = (s32[384]{0:T(512)S(1)}, s32[384]{0:T(512)}, u32[]{:S(2)}) copy-start(s32[384]{0:T(512)} %copy-done.6) | copy-start | bytes 4612
  68.7 5.8 %collective-permute-start.13 = (f32[14,3072]{1,0:T(8,128)S(1)}, f32[14,3072]{1,0:T(8,128)S(1)}, u32[]{:S(2)}, u32[]{:S(2)}) collective-permute-start(f32[14,3072]{1,0:T(8,128)S(1)} %reshape.359), channel_id=1, source_target_pairs={{0,16},{16,0},{1,17},{17,1},{2,18},{18,2},{3,19},{19,3},{4,20},{20... | collective-permute-start | bytes 516104 | tf_op jit(solution)/shard_map/ppermute | solution.py:45
